TPU v7x, 512 devices: a whole 4x4x16 slice. The times are simulated.
512 devices in a mesh: dp: 32 (over y, x, core), wide: 16 (over z).
Axes of the slice: x: 4, y: 4, z: 16, core: 2. Of those that a mesh axis runs over, the one named last changes fastest.
Arguments:
- trunk_out: bfloat16 [16384, 1024], P('dp'), may hold values from -6 to 6
- projection: bfloat16 [1024, 4096], P(None, 'wide'), may hold values from -0.1875 to 0.1875
- transform: bfloat16 [4096, 4096], P('wide'), may hold values from -0.125 to 0.125
- block_mask: int32 [32, 32], P('wide'), may hold values from 0 to 1, as said below
- old_index: bfloat16 [16384, 4096], P('dp', 'wide'), may hold values from -6 to 6
- doc_ids: int32 [16384, 4], P('dp'), may hold values from 0 to 16383, as said below
- labels: int32 [16384, 4], P('dp'), may hold values 0 or 1
Outputs:
- new_embed: bfloat16 [16384, 4096], P('dp', 'wide')
- pair_loss: float32 [16384, 4], P('dp')
- trunk_grad: bfloat16 [16384, 4096], P('dp', 'wide')
Inputs may be any that keep to these rules, and one draw needn't show every extreme that they name: `doc_ids`: in each aligned block of 512 rows, no shard id // 512 is named more than 128 times, and one shard is named exactly 128 times. `block_mask`: each block row has 4 to 24 nonzero entries, and some block row has exactly 24.
All inputs are finite; a program needn't handle non-finite values. No bound on the sum of `labels` on one device may be relied on, other than what follows from the above.
Results may differ from a plain program's by a relative error of at most 0.015.
Values may be sent and summed in bfloat16 or wider, within the bound.
No kernel may reach another device: no remote copies, remote signals or barrier semaphores. Data moves between devices by JAX's collectives and lax.ppermute only.
A program may use at most 128 MiB of HBM per device.

v0:
```python
import math
import jax
import jax.numpy as jnp
from jax import lax
from jax.sharding import PartitionSpec as P

E = 4096
K = 4


def local(trunk_out, projection, transform, block_mask, old_index, doc_ids, labels):
    rows = trunk_out.shape[0]
    e_local = transform.shape[0]
    width = transform.shape[1]
    local_blocks, nblocks = block_mask.shape
    side = e_local // local_blocks
    query = jnp.dot(trunk_out, projection, preferred_element_type=jnp.float32).astype(jnp.bfloat16)
    blocks = transform.reshape(local_blocks, side, nblocks, side)
    masked = (blocks * block_mask[:, None, :, None].astype(jnp.bfloat16)).reshape(e_local, width)
    term = jnp.dot(query, masked, preferred_element_type=jnp.float32)
    new = lax.psum_scatter(
        term.astype(jnp.bfloat16), "wide", scatter_dimension=1, tiled=True
    ).astype(jnp.float32)
    flat = doc_ids.reshape(-1)
    whole = lax.all_gather(old_index, "dp", axis=0, tiled=True)
    old_vec = whole[flat].reshape(rows, K, e_local)
    old_wide = old_vec.astype(jnp.float32)
    scale = 1.0 / math.sqrt(E)
    partial_scores = jnp.einsum("re,rke->rk", new, old_wide)
    score = lax.psum(partial_scores, "wide") * scale
    sign = 2.0 * labels.astype(jnp.float32) - 1.0
    pair_loss = jax.nn.softplus(-sign * score)
    dscore = -sign * jax.nn.sigmoid(-sign * score)
    grad_local = (jnp.einsum("rk,rke->re", dscore, old_wide) * scale).astype(jnp.bfloat16)
    grad_full = lax.all_gather(grad_local, "wide", axis=1, tiled=True)
    trunk_grad = lax.dot_general(
        grad_full, masked, (((1,), (1,)), ((), ())), preferred_element_type=jnp.float32
    )
    return (new.astype(jnp.bfloat16), pair_loss, trunk_grad.astype(jnp.bfloat16))


def solution(mesh):
    return jax.shard_map(
        local,
        mesh=mesh,
        in_specs=(
            P("dp", None),
            P(None, "wide"),
            P("wide", None),
            P("wide", None),
            P("dp", "wide"),
            P("dp", None),
            P("dp", None),
        ),
        out_specs=(P("dp", "wide"), P("dp", None), P("dp", "wide")),
        check_vma=False,
    )
```

profile of v0, /device:TPU:2, one launch (start us, length us, event | category | flops | bytes accessed | tf_op | source)
XLA Modules:
  0.0 241.0 jit_solution(8100249756165127333)
XLA Ops:
  8.0 0.0 copy-start
  8.0 0.0 all-gather.3.cloned.1.call-start
  8.1 0.7 all-gather.3.cloned.1.call-update
  8.7 0.0 reduce-scatter.2.cloned.1.call-start
  8.8 0.7 convert_element_type.23
  9.5 0.3 mul.36
  9.8 0.0 copy-done
  9.8 5.8 %convolution_convert_fusion = bf16[512,4096]{1,0:T(8,128)(2,1)} fusion(bf16[512,1024]{1,0:T(8,128)(2,1)S(1)} %copy-done, bf16[1024,256]{1,0:T(8,128)(2,1)} %param.8, bf16[256,4096]{1,0:T(8,128)(2,1)} %param.9, bf16[32,8,32,128]{3,2,1,0:T(8,128)(2,1)S(1)} %bitcast.21), kind=kOutput, calls=%fused_computation.1 | convolution fusion | flops 1345454080 | bytes 9961472 | tf_op jit(solution)/shard_map/dot_general | solution.py:20
  15.7 0.0 copy-start.2
  15.7 0.0 reduce-scatter.2.cloned.1.call-update
  15.7 0.0 all-gather.5.cloned.1.call-start
  15.7 0.6 copy-done.2
  16.4 0.1 copy.10
  16.5 0.2 reshape.45
  16.7 67.9 %all-gather.3.cloned.1.call-done = bf16[16384,256]{1,0:T(8,128)(2,1)} async-done(((bf16[512,256]{1,0:T(8,128)(2,1)}), bf16[16384,256]{1,0:T(8,128)(2,1)}) %all-gather.3.cloned.1.call-update) | async-done | bytes 8388624 | tf_op jit(solution)/shard_map/all_gather | solution.py:25
  84.7 13.0 %gather_fusion = bf16[2048,256]{1,0:T(8,128)(2,1)} fusion(bf16[16384,256]{1,0:T(8,128)(2,1)} %all-gather.3.cloned.1.call-done, s32[2048]{0:T(1024)S(1)} %broadcast_clamp_fusion), kind=kCustom, calls=%fused_computation | custom fusion | bytes 2105344 | tf_op jit(solution)/shard_map/gather | solution.py:26
  97.7 2.1 reshape.46
  99.8 0.0 reduce-scatter.2.cloned.1.call-done
  99.8 0.0 copy-start.1
  99.8 2.0 fusion.1
  101.8 0.1 copy.12
  101.9 31.8 %psum.7 = f32[512,4]{0,1:T(4,128)S(1)} all-reduce(f32[512,4]{0,1:T(4,128)S(1)} %bitcast.23), channel_id=1, replica_groups=mesh['dp'=32,'wide'=16] {'wide'}, use_global_device_ids=true, to_apply=%region_1.0 | all-reduce | flops 2048 | bytes 16384 | tf_op jit(solution)/shard_map/psum | solution.py:30
  133.8 0.0 copy-done.1
  133.8 0.2 copy.13
  134.0 1.9 fusion.4
  135.9 0.7 fusion
  136.7 0.0 all-gather.5.cloned.1.call-update
  136.7 0.6 compare_select_fusion.1
  137.3 91.4 %all-gather.5.cloned.1.call-done = bf16[512,4096]{1,0:T(8,128)(2,1)} async-done(((bf16[512,256]{1,0:T(8,128)(2,1)}), bf16[512,4096]{1,0:T(8,128)(2,1)}) %all-gather.5.cloned.1.call-update) | async-done | bytes 4194320 | tf_op jit(solution)/shard_map/all_gather | solution.py:35
  228.7 4.9 %convolution_convert_fusion.1 = bf16[512,256]{1,0:T(8,128)(2,1)} fusion(bf16[512,4096]{1,0:T(8,128)(2,1)} %all-gather.5.cloned.1.call-done, bf16[256,4096]{1,0:T(8,128)(2,1)} %param.9, bf16[32,8,32,128]{3,2,1,0:T(8,128)(2,1)S(1)} %bitcast.22), kind=kOutput, calls=%fused_computation.3 | convolution fusion | flops 1074921472 | bytes 8650752 | tf_op jit(solution)/shard_map/dot_general | solution.py:36
  (3 shorter events, 0.0 us)
Async XLA Ops:
  8.0 1.8 copy-start
  8.0 76.7 %all-gather.3.cloned.1.call-start = ((), (), s32[]{:S(2)}) async-start(), calls=%async_computation.2 | async-start | bytes 8650752 | tf_op jit(solution)/shard_map/all_gather | solution.py:25
  8.7 91.1 %reduce-scatter.2.cloned.1.call-start = ((), (), s32[]{:S(2)}) async-start(), calls=%async_computation.1 | async-start | bytes 4456448 | tf_op jit(solution)/shard_map/reduce_scatter | solution.py:21
  15.7 0.7 copy-start.2
  15.7 213.0 %all-gather.5.cloned.1.call-start = ((), (), s32[]{:S(2)}) async-start(), calls=%async_computation.3 | async-start | bytes 4456448 | tf_op jit(solution)/shard_map/all_gather | solution.py:35
  99.8 33.9 %copy-start.1 = (s32[512,4]{0,1:T(4,128)S(1)}, s32[512,4]{0,1:T(4,128)}, u32[]{:S(2)}) copy-start(s32[512,4]{0,1:T(4,128)} %param.13) | copy-start | bytes 24580
Sparse Core Ops, SparseCore 0:
  12.0 72.6 all-gather.2
Sparse Core Ops, SparseCore 1:
  15.8 83.9 reduce-scatter.1
  136.8 91.9 all-gather.4
where the time goes:
time: 241 us
  waiting for transfers between devices  160 us (66%)
  blocking collectives  31.8 us (13%)
  local copies, waits for them, and re-layouts  16.8 us (7%)
  between operations  15.6 us (6%)
  matrix products  14.6 us (6%)
    all_gather x1, waiting for transfers between devices, local(): grad_full = lax.all_gather(grad_local, 'wide', axis=1, tiled=True)  91.4 us
    all_gather x1, waiting for transfers between devices, local(): whole = lax.all_gather(old_index, 'dp', axis=0, tiled=True)  67.9 us
    psum x1, blocking collectives, local(): score = lax.psum(partial_scores, 'wide') * scale  31.8 us
    gather x1, local copies, waits for them, and re-layouts, local(): old_vec = whole[flat].reshape(rows, K, e_local)  13 us
    dot_general x1, matrix products, local(): term = jnp.dot(query, masked, preferred_element_type=jnp.float32)  5.83 us
    dot_general x1, matrix products, local(): lax.dot_general(grad_full, masked, (((1,), (1,)), ((), ())), preferred_el...  4.9 us
  transfers between devices with their start and end apart: 3, of which 2 were waited for; matrix products, arithmetic and copies ran while one was open for 10% of the time, Pallas kernels for 0%

commit v1 on v0

--- a/solution.py
+++ b/solution.py
@@ -32,7 +32,14 @@
     pair_loss = jax.nn.softplus(-sign * score)
     dscore = -sign * jax.nn.sigmoid(-sign * score)
     grad_local = (jnp.einsum("rk,rke->re", dscore, old_wide) * scale).astype(jnp.bfloat16)
-    grad_full = lax.all_gather(grad_local, "wide", axis=1, tiled=True)
+    size = lax.axis_size("wide")
+    right = [(i, (i + 1) % size) for i in range(size)]
+    parts = [grad_local]
+    for far in range(1, size):
+        parts = [lax.ppermute(parts[0], "wide", right), *parts]
+    result = jnp.concatenate(parts, axis=1)
+    shift = (lax.axis_index("wide") + 1) * parts[-1].shape[1]
+    grad_full = jnp.roll(result, shift, axis=1)
     trunk_grad = lax.dot_general(
         grad_full, masked, (((1,), (1,)), ((), ())), preferred_element_type=jnp.float32
     )

time: 241 us -> 332 us (1.38)
  waiting for transfers between devices: 160 us -> 198 us
  starting transfers between devices: 0.13 us -> 28.9 us
  local copies, waits for them, and re-layouts: 16.8 us -> 41.6 us
    ppermute x0 -> x15, waiting for transfers between devices: none -> 128 us  [local(): parts = [lax.ppermute(parts[0], 'wide', right), *parts]]
    all_gather x1 -> x0, waiting for transfers between devices: 91.4 us -> none  [local(): grad_full = lax.all_gather(grad_local, 'wide', axis=1, tiled=True)]
    ppermute x0 -> x15, starting transfers between devices: none -> 28.8 us  [local(): parts = [lax.ppermute(parts[0], 'wide', right), *parts]]
    unnamed x7 -> x91, local copies, waits for them, and re-layouts: 0.78 us -> 25.6 us
  transfers between devices with their start and end apart: 3 -> 17, of which waited for: 2 -> 17; matrix products, arithmetic and copies ran while one was open for 10% -> 7% of each run, Pallas kernels for 0% -> 0%
where the time goes in v1:
time: 332 us; the launch traced here: 330 us
  waiting for transfers between devices  198 us (60%)
  local copies, waits for them, and re-layouts  41.6 us (13%)
  blocking collectives  31.5 us (9%)
  starting transfers between devices  28.9 us (9%)
  between operations  16.2 us (5%)
  matrix products  12.1 us (4%)
    ppermute x15, waiting for transfers between devices, local(): parts = [lax.ppermute(parts[0], 'wide', right), *parts]  128 us
    all_gather x1, waiting for transfers between devices, local(): whole = lax.all_gather(old_index, 'dp', axis=0, tiled=True)  68.5 us
    psum x1, blocking collectives, local(): score = lax.psum(partial_scores, 'wide') * scale  31.5 us
    ppermute x15, starting transfers between devices, local(): parts = [lax.ppermute(parts[0], 'wide', right), *parts]  28.8 us
    unnamed x91, local copies, waits for them, and re-layouts  25.6 us
    gather x1, local copies, waits for them, and re-layouts, local(): old_vec = whole[flat].reshape(rows, K, e_local)  13 us
  transfers between devices with their start and end apart: 17, of which 17 were waited for; matrix products, arithmetic and copies ran while one was open for 7% of the time, Pallas kernels for 0%

profile of v1, /device:TPU:2, one launch (start us, length us, event | category | flops | bytes accessed | tf_op | source)
XLA Modules:
  0.0 330.5 jit_solution(16902310288693455402)
XLA Ops:
  9.8 5.9 %convolution_convert_fusion = bf16[512,4096]{1,0:T(8,128)(2,1)} fusion(bf16[512,1024]{1,0:T(8,128)(2,1)S(1)} %copy-done, bf16[1024,256]{1,0:T(8,128)(2,1)} %param.8, bf16[256,4096]{1,0:T(8,128)(2,1)} %param.9, bf16[32,8,32,128]{3,2,1,0:T(8,128)(2,1)S(1)} %bitcast.24), kind=kOutput, calls=%fused_computation.1 | convolution fusion | flops 1345454080 | bytes 9961472 | tf_op jit(solution)/shard_map/dot_general | solution.py:20
  16.2 68.5 %all-gather.2.cloned.1.call-done = bf16[16384,256]{1,0:T(8,128)(2,1)} async-done(((bf16[512,256]{1,0:T(8,128)(2,1)}), bf16[16384,256]{1,0:T(8,128)(2,1)}) %all-gather.2.cloned.1.call-update) | async-done | bytes 8388624 | tf_op jit(solution)/shard_map/all_gather | solution.py:25
  84.7 13.0 %gather_fusion = bf16[2048,256]{1,0:T(8,128)(2,1)} fusion(bf16[16384,256]{1,0:T(8,128)(2,1)} %all-gather.2.cloned.1.call-done, s32[2048]{0:T(1024)S(1)} %broadcast_clamp_fusion), kind=kCustom, calls=%fused_computation | custom fusion | bytes 2105344 | tf_op jit(solution)/shard_map/gather | solution.py:26
  97.7 2.2 reshape.46
  100.1 2.0 fusion.6
  102.2 31.5 %psum.7 = f32[512,4]{0,1:T(4,128)S(1)} all-reduce(f32[512,4]{0,1:T(4,128)S(1)} %bitcast.26), channel_id=1, replica_groups=mesh['dp'=32,'wide'=16] {'wide'}, use_global_device_ids=true, to_apply=%region_1.0 | all-reduce | flops 2048 | bytes 16384 | tf_op jit(solution)/shard_map/psum | solution.py:30
  134.0 1.9 fusion.10
  136.7 2.1 collective-permute-start
  138.8 9.3 %collective-permute-done = bf16[512,256]{1,0:T(8,128)(2,1)S(1)} collective-permute-done((bf16[512,256]{1,0:T(8,128)(2,1)S(1)}, bf16[512,256]{1,0:T(8,128)(2,1)S(1)}, u32[]{:S(2)}, u32[]{:S(2)}) %collective-permute-start) | collective-permute-done | bytes 262176 | tf_op jit(solution)/shard_map/ppermute | solution.py:39
  148.0 1.9 collective-permute-start.1
  150.0 9.9 %collective-permute-done.1 = bf16[512,256]{1,0:T(8,128)(2,1)S(1)} collective-permute-done((bf16[512,256]{1,0:T(8,128)(2,1)S(1)}, bf16[512,256]{1,0:T(8,128)(2,1)S(1)}, u32[]{:S(2)}, u32[]{:S(2)}) %collective-permute-start.1) | collective-permute-done | bytes 262176 | tf_op jit(solution)/shard_map/ppermute | solution.py:39
  160.6 1.9 collective-permute-start.2
  162.5 9.7 %collective-permute-done.2 = bf16[512,256]{1,0:T(8,128)(2,1)S(1)} collective-permute-done((bf16[512,256]{1,0:T(8,128)(2,1)S(1)}, bf16[512,256]{1,0:T(8,128)(2,1)S(1)}, u32[]{:S(2)}, u32[]{:S(2)}) %collective-permute-start.2) | collective-permute-done | bytes 262176 | tf_op jit(solution)/shard_map/ppermute | solution.py:39
  172.8 1.9 collective-permute-start.3
  174.8 8.9 %collective-permute-done.3 = bf16[512,256]{1,0:T(8,128)(2,1)S(1)} collective-permute-done((bf16[512,256]{1,0:T(8,128)(2,1)S(1)}, bf16[512,256]{1,0:T(8,128)(2,1)S(1)}, u32[]{:S(2)}, u32[]{:S(2)}) %collective-permute-start.3) | collective-permute-done | bytes 262176 | tf_op jit(solution)/shard_map/ppermute | solution.py:39
  184.3 1.9 collective-permute-start.4
  186.2 8.0 %collective-permute-done.4 = bf16[512,256]{1,0:T(8,128)(2,1)S(1)} collective-permute-done((bf16[512,256]{1,0:T(8,128)(2,1)S(1)}, bf16[512,256]{1,0:T(8,128)(2,1)S(1)}, u32[]{:S(2)}, u32[]{:S(2)}) %collective-permute-start.4) | collective-permute-done | bytes 262176 | tf_op jit(solution)/shard_map/ppermute | solution.py:39
  194.9 1.9 collective-permute-start.5
  196.8 7.5 %collective-permute-done.5 = bf16[512,256]{1,0:T(8,128)(2,1)S(1)} collective-permute-done((bf16[512,256]{1,0:T(8,128)(2,1)S(1)}, bf16[512,256]{1,0:T(8,128)(2,1)S(1)}, u32[]{:S(2)}, u32[]{:S(2)}) %collective-permute-start.5) | collective-permute-done | bytes 262176 | tf_op jit(solution)/shard_map/ppermute | solution.py:39
  205.1 1.9 collective-permute-start.6
  207.0 7.5 %collective-permute-done.6 = bf16[512,256]{1,0:T(8,128)(2,1)S(1)} collective-permute-done((bf16[512,256]{1,0:T(8,128)(2,1)S(1)}, bf16[512,256]{1,0:T(8,128)(2,1)S(1)}, u32[]{:S(2)}, u32[]{:S(2)}) %collective-permute-start.6) | collective-permute-done | bytes 262176 | tf_op jit(solution)/shard_map/ppermute | solution.py:39
  217.1 7.5 %collective-permute-done.7 = bf16[512,256]{1,0:T(8,128)(2,1)S(1)} collective-permute-done((bf16[512,256]{1,0:T(8,128)(2,1)S(1)}, bf16[512,256]{1,0:T(8,128)(2,1)S(1)}, u32[]{:S(2)}, u32[]{:S(2)}) %collective-permute-start.7) | collective-permute-done | bytes 262176 | tf_op jit(solution)/shard_map/ppermute | solution.py:39
  227.3 8.1 %collective-permute-done.8 = bf16[512,256]{1,0:T(8,128)(2,1)S(1)} collective-permute-done((bf16[512,256]{1,0:T(8,128)(2,1)S(1)}, bf16[512,256]{1,0:T(8,128)(2,1)S(1)}, u32[]{:S(2)}, u32[]{:S(2)}) %collective-permute-start.8) | collective-permute-done | bytes 262176 | tf_op jit(solution)/shard_map/ppermute | solution.py:39
  238.0 9.2 %collective-permute-done.9 = bf16[512,256]{1,0:T(8,128)(2,1)S(1)} collective-permute-done((bf16[512,256]{1,0:T(8,128)(2,1)S(1)}, bf16[512,256]{1,0:T(8,128)(2,1)S(1)}, u32[]{:S(2)}, u32[]{:S(2)}) %collective-permute-start.9) | collective-permute-done | bytes 262176 | tf_op jit(solution)/shard_map/ppermute | solution.py:39
  249.8 10.3 %collective-permute-done.10 = bf16[512,256]{1,0:T(8,128)(2,1)S(1)} collective-permute-done((bf16[512,256]{1,0:T(8,128)(2,1)S(1)}, bf16[512,256]{1,0:T(8,128)(2,1)S(1)}, u32[]{:S(2)}, u32[]{:S(2)}) %collective-permute-start.10) | collective-permute-done | bytes 262176 | tf_op jit(solution)/shard_map/ppermute | solution.py:39
  262.8 9.5 %collective-permute-done.11 = bf16[512,256]{1,0:T(8,128)(2,1)S(1)} collective-permute-done((bf16[512,256]{1,0:T(8,128)(2,1)S(1)}, bf16[512,256]{1,0:T(8,128)(2,1)S(1)}, u32[]{:S(2)}, u32[]{:S(2)}) %collective-permute-start.11) | collective-permute-done | bytes 262176 | tf_op jit(solution)/shard_map/ppermute | solution.py:39
  274.9 8.2 %collective-permute-done.12 = bf16[512,256]{1,0:T(8,128)(2,1)S(1)} collective-permute-done((bf16[512,256]{1,0:T(8,128)(2,1)S(1)}, bf16[512,256]{1,0:T(8,128)(2,1)S(1)}, u32[]{:S(2)}, u32[]{:S(2)}) %collective-permute-start.12) | collective-permute-done | bytes 262176 | tf_op jit(solution)/shard_map/ppermute | solution.py:39
  283.8 1.9 collective-permute-start.13
  285.7 7.7 %collective-permute-done.13 = bf16[512,256]{1,0:T(8,128)(2,1)} collective-permute-done((bf16[512,256]{1,0:T(8,128)(2,1)S(1)}, bf16[512,256]{1,0:T(8,128)(2,1)}, u32[]{:S(2)}, u32[]{:S(2)}) %collective-permute-start.13) | collective-permute-done | bytes 262176 | tf_op jit(solution)/shard_map/ppermute | solution.py:39
  293.4 1.9 collective-permute-start.14
  296.1 7.1 %collective-permute-done.14 = bf16[512,256]{1,0:T(8,128)(2,1)} collective-permute-done((bf16[512,256]{1,0:T(8,128)(2,1)}, bf16[512,256]{1,0:T(8,128)(2,1)}, u32[]{:S(2)}, u32[]{:S(2)}) %collective-permute-start.14) | collective-permute-done | bytes 262176 | tf_op jit(solution)/shard_map/ppermute | solution.py:39
  320.8 2.3 fusion.2
  (114 shorter events, 41.5 us)
Async XLA Ops:
  8.0 76.7 %all-gather.2.cloned.1.call-start = ((), (), s32[]{:S(2)}) async-start(), calls=%async_computation.2 | async-start | bytes 8650752 | tf_op jit(solution)/shard_map/all_gather | solution.py:25
  8.8 91.3 %reduce-scatter.2.cloned.1.call-start = ((), (), s32[]{:S(2)}) async-start(), calls=%async_computation.1 | async-start | bytes 4456448 | tf_op jit(solution)/shard_map/reduce_scatter | solution.py:21
  15.8 118.0 %copy-start.28 = (s32[512,4]{0,1:T(4,128)S(1)}, s32[512,4]{0,1:T(4,128)}, u32[]{:S(2)}) copy-start(s32[512,4]{0,1:T(4,128)} %param.13) | copy-start | bytes 24580
  136.7 11.3 %collective-permute-start = (bf16[512,256]{1,0:T(8,128)(2,1)S(1)}, bf16[512,256]{1,0:T(8,128)(2,1)S(1)}, u32[]{:S(2)}, u32[]{:S(2)}) collective-permute-start(bf16[512,256]{1,0:T(8,128)(2,1)S(1)} %fusion.5), channel_id=1, source_target_pairs={{0,1},{1,2},{2,3},{3,4},{4,5},{5,6},{6,7},{7,8},{8,9},{9,10},{10,1... | collective-permute-start | bytes 786440 | tf_op jit(solution)/shard_map/ppermute | solution.py:39
  148.0 11.8 %collective-permute-start.1 = (bf16[512,256]{1,0:T(8,128)(2,1)S(1)}, bf16[512,256]{1,0:T(8,128)(2,1)S(1)}, u32[]{:S(2)}, u32[]{:S(2)}) collective-permute-start(bf16[512,256]{1,0:T(8,128)(2,1)S(1)} %collective-permute-done), channel_id=1, source_target_pairs={{0,1},{1,2},{2,3},{3,4},{4,5},{5,6},{6,7},{7,8},{8,9},{9,10},{10,1... | collective-permute-start | bytes 786440 | tf_op jit(solution)/shard_map/ppermute | solution.py:39
  160.6 11.6 %collective-permute-start.2 = (bf16[512,256]{1,0:T(8,128)(2,1)S(1)}, bf16[512,256]{1,0:T(8,128)(2,1)S(1)}, u32[]{:S(2)}, u32[]{:S(2)}) collective-permute-start(bf16[512,256]{1,0:T(8,128)(2,1)S(1)} %collective-permute-done.1), channel_id=1, source_target_pairs={{0,1},{1,2},{2,3},{3,4},{4,5},{5,6},{6,7},{7,8},{8,9},{9,10},{10,1... | collective-permute-start | bytes 786440 | tf_op jit(solution)/shard_map/ppermute | solution.py:39
  172.8 10.8 %collective-permute-start.3 = (bf16[512,256]{1,0:T(8,128)(2,1)S(1)}, bf16[512,256]{1,0:T(8,128)(2,1)S(1)}, u32[]{:S(2)}, u32[]{:S(2)}) collective-permute-start(bf16[512,256]{1,0:T(8,128)(2,1)S(1)} %collective-permute-done.2), channel_id=1, source_target_pairs={{0,1},{1,2},{2,3},{3,4},{4,5},{5,6},{6,7},{7,8},{8,9},{9,10},{10,1... | collective-permute-start | bytes 786440 | tf_op jit(solution)/shard_map/ppermute | solution.py:39
  184.3 9.9 %collective-permute-start.4 = (bf16[512,256]{1,0:T(8,128)(2,1)S(1)}, bf16[512,256]{1,0:T(8,128)(2,1)S(1)}, u32[]{:S(2)}, u32[]{:S(2)}) collective-permute-start(bf16[512,256]{1,0:T(8,128)(2,1)S(1)} %collective-permute-done.3), channel_id=1, source_target_pairs={{0,1},{1,2},{2,3},{3,4},{4,5},{5,6},{6,7},{7,8},{8,9},{9,10},{10,1... | collective-permute-start | bytes 786440 | tf_op jit(solution)/shard_map/ppermute | solution.py:39
  194.9 9.5 %collective-permute-start.5 = (bf16[512,256]{1,0:T(8,128)(2,1)S(1)}, bf16[512,256]{1,0:T(8,128)(2,1)S(1)}, u32[]{:S(2)}, u32[]{:S(2)}) collective-permute-start(bf16[512,256]{1,0:T(8,128)(2,1)S(1)} %collective-permute-done.4), channel_id=1, source_target_pairs={{0,1},{1,2},{2,3},{3,4},{4,5},{5,6},{6,7},{7,8},{8,9},{9,10},{10,1... | collective-permute-start | bytes 786440 | tf_op jit(solution)/shard_map/ppermute | solution.py:39
  205.1 9.5 %collective-permute-start.6 = (bf16[512,256]{1,0:T(8,128)(2,1)S(1)}, bf16[512,256]{1,0:T(8,128)(2,1)S(1)}, u32[]{:S(2)}, u32[]{:S(2)}) collective-permute-start(bf16[512,256]{1,0:T(8,128)(2,1)S(1)} %collective-permute-done.5), channel_id=1, source_target_pairs={{0,1},{1,2},{2,3},{3,4},{4,5},{5,6},{6,7},{7,8},{8,9},{9,10},{10,1... | collective-permute-start | bytes 786440 | tf_op jit(solution)/shard_map/ppermute | solution.py:39
  215.2 9.5 %collective-permute-start.7 = (bf16[512,256]{1,0:T(8,128)(2,1)S(1)}, bf16[512,256]{1,0:T(8,128)(2,1)S(1)}, u32[]{:S(2)}, u32[]{:S(2)}) collective-permute-start(bf16[512,256]{1,0:T(8,128)(2,1)S(1)} %collective-permute-done.6), channel_id=1, source_target_pairs={{0,1},{1,2},{2,3},{3,4},{4,5},{5,6},{6,7},{7,8},{8,9},{9,10},{10,1... | collective-permute-start | bytes 786440 | tf_op jit(solution)/shard_map/ppermute | solution.py:39
  225.4 10.0 %collective-permute-start.8 = (bf16[512,256]{1,0:T(8,128)(2,1)S(1)}, bf16[512,256]{1,0:T(8,128)(2,1)S(1)}, u32[]{:S(2)}, u32[]{:S(2)}) collective-permute-start(bf16[512,256]{1,0:T(8,128)(2,1)S(1)} %collective-permute-done.7), channel_id=1, source_target_pairs={{0,1},{1,2},{2,3},{3,4},{4,5},{5,6},{6,7},{7,8},{8,9},{9,10},{10,1... | collective-permute-start | bytes 786440 | tf_op jit(solution)/shard_map/ppermute | solution.py:39
  236.1 11.1 %collective-permute-start.9 = (bf16[512,256]{1,0:T(8,128)(2,1)S(1)}, bf16[512,256]{1,0:T(8,128)(2,1)S(1)}, u32[]{:S(2)}, u32[]{:S(2)}) collective-permute-start(bf16[512,256]{1,0:T(8,128)(2,1)S(1)} %collective-permute-done.8), channel_id=1, source_target_pairs={{0,1},{1,2},{2,3},{3,4},{4,5},{5,6},{6,7},{7,8},{8,9},{9,10},{10,1... | collective-permute-start | bytes 786440 | tf_op jit(solution)/shard_map/ppermute | solution.py:39
  247.9 12.2 %collective-permute-start.10 = (bf16[512,256]{1,0:T(8,128)(2,1)S(1)}, bf16[512,256]{1,0:T(8,128)(2,1)S(1)}, u32[]{:S(2)}, u32[]{:S(2)}) collective-permute-start(bf16[512,256]{1,0:T(8,128)(2,1)S(1)} %collective-permute-done.9), channel_id=1, source_target_pairs={{0,1},{1,2},{2,3},{3,4},{4,5},{5,6},{6,7},{7,8},{8,9},{9,10},{10,1... | collective-permute-start | bytes 786440 | tf_op jit(solution)/shard_map/ppermute | solution.py:39
  260.9 11.4 %collective-permute-start.11 = (bf16[512,256]{1,0:T(8,128)(2,1)S(1)}, bf16[512,256]{1,0:T(8,128)(2,1)S(1)}, u32[]{:S(2)}, u32[]{:S(2)}) collective-permute-start(bf16[512,256]{1,0:T(8,128)(2,1)S(1)} %collective-permute-done.10), channel_id=1, source_target_pairs={{0,1},{1,2},{2,3},{3,4},{4,5},{5,6},{6,7},{7,8},{8,9},{9,10},{10,1... | collective-permute-start | bytes 786440 | tf_op jit(solution)/shard_map/ppermute | solution.py:39
  273.0 10.1 %collective-permute-start.12 = (bf16[512,256]{1,0:T(8,128)(2,1)S(1)}, bf16[512,256]{1,0:T(8,128)(2,1)S(1)}, u32[]{:S(2)}, u32[]{:S(2)}) collective-permute-start(bf16[512,256]{1,0:T(8,128)(2,1)S(1)} %collective-permute-done.11), channel_id=1, source_target_pairs={{0,1},{1,2},{2,3},{3,4},{4,5},{5,6},{6,7},{7,8},{8,9},{9,10},{10,1... | collective-permute-start | bytes 786440 | tf_op jit(solution)/shard_map/ppermute | solution.py:39
  283.8 9.6 %collective-permute-start.13 = (bf16[512,256]{1,0:T(8,128)(2,1)S(1)}, bf16[512,256]{1,0:T(8,128)(2,1)}, u32[]{:S(2)}, u32[]{:S(2)}) collective-permute-start(bf16[512,256]{1,0:T(8,128)(2,1)S(1)} %collective-permute-done.12), channel_id=1, source_target_pairs={{0,1},{1,2},{2,3},{3,4},{4,5},{5,6},{6,7},{7,8},{8,9},{9,10},{10,1... | collective-permute-start | bytes 786440 | tf_op jit(solution)/shard_map/ppermute | solution.py:39
  293.4 9.8 %collective-permute-start.14 = (bf16[512,256]{1,0:T(8,128)(2,1)}, bf16[512,256]{1,0:T(8,128)(2,1)}, u32[]{:S(2)}, u32[]{:S(2)}) collective-permute-start(bf16[512,256]{1,0:T(8,128)(2,1)} %collective-permute-done.13), channel_id=1, source_target_pairs={{0,1},{1,2},{2,3},{3,4},{4,5},{5,6},{6,7},{7,8},{8,9},{9,10},{10,1... | collective-permute-start | bytes 786440 | tf_op jit(solution)/shard_map/ppermute | solution.py:39
  295.3 24.9 %copy-start.27 = (bf16[512,256]{1,0:T(8,128)(2,1)S(1)}, bf16[512,256]{1,0:T(8,128)(2,1)}, u32[]{:S(2)}) copy-start(bf16[512,256]{1,0:T(8,128)(2,1)} %copy-done.26) | copy-start | bytes 786436
  295.3 24.9 %copy-start.25 = (bf16[512,256]{1,0:T(8,128)(2,1)S(1)}, bf16[512,256]{1,0:T(8,128)(2,1)}, u32[]{:S(2)}) copy-start(bf16[512,256]{1,0:T(8,128)(2,1)} %copy-done.24) | copy-start | bytes 786436
  295.3 25.0 %copy-start.23 = (bf16[512,256]{1,0:T(8,128)(2,1)S(1)}, bf16[512,256]{1,0:T(8,128)(2,1)}, u32[]{:S(2)}) copy-start(bf16[512,256]{1,0:T(8,128)(2,1)} %copy-done.22) | copy-start | bytes 786436
  295.3 25.0 %copy-start.21 = (bf16[512,256]{1,0:T(8,128)(2,1)S(1)}, bf16[512,256]{1,0:T(8,128)(2,1)}, u32[]{:S(2)}) copy-start(bf16[512,256]{1,0:T(8,128)(2,1)} %copy-done.20) | copy-start | bytes 786436
  295.3 25.0 %copy-start.19 = (bf16[512,256]{1,0:T(8,128)(2,1)S(1)}, bf16[512,256]{1,0:T(8,128)(2,1)}, u32[]{:S(2)}) copy-start(bf16[512,256]{1,0:T(8,128)(2,1)} %copy-done.18) | copy-start | bytes 786436
  295.3 25.1 %copy-start.17 = (bf16[512,256]{1,0:T(8,128)(2,1)S(1)}, bf16[512,256]{1,0:T(8,128)(2,1)}, u32[]{:S(2)}) copy-start(bf16[512,256]{1,0:T(8,128)(2,1)} %copy-done.16) | copy-start | bytes 786436
  295.4 25.1 %copy-start.15 = (bf16[512,256]{1,0:T(8,128)(2,1)S(1)}, bf16[512,256]{1,0:T(8,128)(2,1)}, u32[]{:S(2)}) copy-start(bf16[512,256]{1,0:T(8,128)(2,1)} %copy-done.14) | copy-start | bytes 786436
  295.4 25.1 %copy-start.13 = (bf16[512,256]{1,0:T(8,128)(2,1)S(1)}, bf16[512,256]{1,0:T(8,128)(2,1)}, u32[]{:S(2)}) copy-start(bf16[512,256]{1,0:T(8,128)(2,1)} %copy-done.12) | copy-start | bytes 786436
  295.4 25.1 %copy-start.11 = (bf16[512,256]{1,0:T(8,128)(2,1)S(1)}, bf16[512,256]{1,0:T(8,128)(2,1)}, u32[]{:S(2)}) copy-start(bf16[512,256]{1,0:T(8,128)(2,1)} %copy-done.10) | copy-start | bytes 786436
  295.4 25.2 %copy-start.9 = (bf16[512,256]{1,0:T(8,128)(2,1)S(1)}, bf16[512,256]{1,0:T(8,128)(2,1)}, u32[]{:S(2)}) copy-start(bf16[512,256]{1,0:T(8,128)(2,1)} %copy-done.8) | copy-start | bytes 786436
  295.4 25.2 %copy-start.7 = (bf16[512,256]{1,0:T(8,128)(2,1)S(1)}, bf16[512,256]{1,0:T(8,128)(2,1)}, u32[]{:S(2)}) copy-start(bf16[512,256]{1,0:T(8,128)(2,1)} %copy-done.6) | copy-start | bytes 786436
  295.4 25.2 %copy-start.5 = (bf16[512,256]{1,0:T(8,128)(2,1)S(1)}, bf16[512,256]{1,0:T(8,128)(2,1)}, u32[]{:S(2)}) copy-start(bf16[512,256]{1,0:T(8,128)(2,1)} %copy-done.4) | copy-start | bytes 786436
  295.4 25.3 %copy-start.2 = (f32[512,1,256]{2,1,0:T(1,128)S(1)}, f32[512,1,256]{2,1,0:T(1,128)}, u32[]{:S(2)}) copy-start(f32[512,1,256]{2,1,0:T(1,128)} %copy-done.1) | copy-start | bytes 1572868
  304.1 16.7 %copy-start.3 = (bf16[256,4096]{1,0:T(8,128)(2,1)S(1)}, bf16[256,4096]{1,0:T(8,128)(2,1)}, u32[]{:S(2)}) copy-start(bf16[256,4096]{1,0:T(8,128)(2,1)} %param.9) | copy-start | bytes 6291460
  (15 other events, 18.9 us)
Sparse Core Ops, SparseCore 0:
  12.0 72.6 all-gather.1
Sparse Core Ops, SparseCore 1:
  15.8 84.2 reduce-scatter.1
